TPU v7x, 128 devices: a whole 4x4x4 slice. The times are simulated.
128 devices in a mesh: seq: 32 (over z, y, core), tp: 4 (over x).
Axes of the slice: x: 4, y: 4, z: 4, core: 2. Of those that a mesh axis runs over, the one named last changes fastest.
Arguments:
- hidden: bfloat16 [32768, 2048], P('seq', 'tp'), may hold values from -6 to 6
- x_weight: bfloat16 [2048, 4096], P(None, 'tp'), may hold values from -0.125 to 0.125
- z_weight: bfloat16 [2048, 4096], P(None, 'tp'), may hold values from -0.125 to 0.125
- bc_weight: bfloat16 [2048, 256], P(None, 'tp'), may hold values from -0.125 to 0.125
- dt_weight: bfloat16 [2048, 64], P(None, 'tp'), may hold values from -0.125 to 0.125
- conv_x: float32 [4, 4096], P(None, 'tp'), may hold values from -3 to 3
- conv_bc: float32 [4, 256], replicated, may hold values from -3 to 3
- dt_bias: float32 [64], P('tp'), may hold values from -2 to 1
- decay_rate: float32 [64], P('tp'), may hold values from 2e-05 to 0.2
- skip_gain: float32 [64], P('tp'), may hold values from 0.2 to 1.5
- norm_gain: float32 [4096], P('tp'), may hold values from 0.5 to 1.5
- out_weight: bfloat16 [4096, 2048], P('tp'), may hold values from -0.09375 to 0.09375
- lengths: int32 [4], replicated, may hold values from 1 to 16384, as said below
- owners: int32 [32], P('seq'), may hold values from 0 to 3, as said below
Outputs:
- mixed: bfloat16 [32768, 2048], P('seq', 'tp')
- final_state: float32 [32, 64, 64, 128], P('seq', 'tp')
- conv_edge_x: bfloat16 [32, 3, 4096], P('seq', None, 'tp')
- conv_edge_bc: bfloat16 [32, 3, 256], P('seq')
Inputs may be any that keep to these rules, and one draw needn't show every extreme that they name: The prompts are packed in order and their lengths sum to 32768; the second prompt is the longest and holds exactly half of 32768 tokens; the third and fourth together hold at least 3 tokens, and one of them holds one or two. `owners`: every prompt is kept by the same number of indices.
All inputs are finite; a program needn't handle non-finite values.
Results may differ from a plain program's by a relative error of at most 0.013.
Values may be sent and summed in bfloat16 or wider, within the bound.
No kernel may reach another device: no remote copies, remote signals or barrier semaphores. Data moves between devices by JAX's collectives and lax.ppermute only.
A program may use at most 192 MiB of HBM per device.

v0:
```python
import jax
import jax.numpy as jnp
from jax import lax
from jax.sharding import PartitionSpec as P

NS = 128
KCONV = 4
GROUP = 256
PROMPTS = 4
DIN = 4096
highest = lax.Precision.HIGHEST
epsilon = 1e-05


def passed_along(block, axis, distance):
    devices = range(lax.axis_size(axis))
    route = [(i - distance, i) for i in devices if i - distance in devices]
    return lax.ppermute(block, axis, route)


def prefix(value, axis, join, neutral):
    count, mine = (lax.axis_size(axis), lax.axis_index(axis))
    pieces = jax.tree.map(lambda part: lax.all_gather(part, axis), value)
    running = jax.tree.map(
        lambda part, zero: jnp.full_like(part, 0) + jnp.asarray(zero, part.dtype), value, neutral
    )

    def lap(position, running):
        longer = join(running, jax.tree.map(lambda part: part[position], pieces))
        return jax.tree.map(lambda new, old: jnp.where(position < mine, new, old), longer, running)

    return lax.fori_loop(0, count - 1, lap, running)


def segment_of(positions, prompt_end):
    counted = jnp.sum((positions[:, None] >= prompt_end[None, :]).astype(jnp.int32), axis=1)
    return jnp.where(positions < 0, -1, counted)


def short_conv(extended, seg_ext, kernel):
    taps = kernel.shape[0]
    count = extended.shape[0] - taps + 1
    total = jnp.zeros((count, extended.shape[1]), jnp.float32)
    for offset in range(taps):
        same = (seg_ext[offset : offset + count] == seg_ext[taps - 1 :]).astype(jnp.float32)
        total = (
            total
            + extended[offset : offset + count].astype(jnp.float32)
            * kernel[offset][None, :]
            * same[:, None]
        )
    return jax.nn.silu(total).astype(jnp.bfloat16)


def advance_block(state, block):
    x_blk, b_blk, c_blk, dt_blk, log_blk, seg_blk, seg_prior = block
    length = seg_blk.shape[0]
    acum = jnp.cumsum(log_blk, axis=0)
    index = jnp.arange(length, dtype=jnp.int32)
    keep = (seg_blk[:, None] == seg_blk[None, :]) & (index[:, None] >= index[None, :])
    spread = acum[:, None, :] - acum[None, :, :]
    decay = jnp.where(keep[:, :, None], jnp.exp(jnp.where(keep[:, :, None], spread, 0.0)), 0.0)
    scores = jnp.dot(c_blk, b_blk.T, precision=highest)
    mixing = scores[:, :, None] * decay * dt_blk[None, :, :]
    output = jnp.einsum("ijh,jhp->ihp", mixing, x_blk, precision=highest)
    inflow = jnp.where((seg_blk == seg_prior)[:, None], jnp.exp(acum), 0.0)
    output = output + inflow[:, :, None] * jnp.einsum(
        "in,hpn->ihp", c_blk, state, precision=highest
    )
    closing = seg_blk[length - 1]
    tail = (
        jnp.where((seg_blk == closing)[:, None], jnp.exp(acum[length - 1][None, :] - acum), 0.0)
        * dt_blk
    )
    fresh = jnp.einsum("jh,jhp,jn->hpn", tail, x_blk, b_blk, precision=highest)
    carry = jnp.where(closing == seg_prior, jnp.exp(acum[length - 1]), 0.0)
    return (carry[:, None, None] * state + fresh, (output, state))


def state_at(start_state, seg_prior, x_rows, b_rows, dt_rows, log_rows, seg_rows, inner, prompt):
    acum = jnp.cumsum(log_rows, axis=0)
    level = acum[inner]
    index = jnp.arange(seg_rows.shape[0], dtype=jnp.int32)
    chosen = (seg_rows == prompt) & (index <= inner)
    weight = (
        jnp.where(
            chosen[:, None], jnp.exp(jnp.where(chosen[:, None], level[None, :] - acum, 0.0)), 0.0
        )
        * dt_rows
    )
    inflow = jnp.where(seg_rows[inner] == seg_prior, jnp.exp(level), 0.0)
    return inflow[:, None, None] * start_state + jnp.einsum(
        "jh,jhp,jn->hpn", weight, x_rows, b_rows, precision=highest
    )


def per_device(
    hidden,
    x_weight,
    z_weight,
    bc_weight,
    dt_weight,
    conv_x,
    conv_bc,
    dt_bias,
    decay_rate,
    skip_gain,
    norm_gain,
    out_weight,
    lengths,
    owners,
):
    rows_here = hidden.shape[0]
    width_here = x_weight.shape[1]
    heads_here = dt_bias.shape[0]
    head_width = width_here // heads_here
    my_index = lax.axis_index("seq")
    first_row = my_index * rows_here
    prompt_end = jnp.cumsum(lengths)
    prompt_start = prompt_end - lengths
    positions = first_row + jnp.arange(rows_here, dtype=jnp.int32)
    segment = segment_of(positions, prompt_end)
    bc_full = lax.all_gather(bc_weight, "tp", axis=1, tiled=True)
    piece = lax.all_gather(hidden, "tp", axis=1, tiled=True)

    def take(matrix):
        return jnp.dot(piece, matrix, preferred_element_type=jnp.float32)

    x_acc = take(x_weight)
    z_acc = take(z_weight)
    dt_raw = take(dt_weight)
    bc_acc = take(bc_full)
    x_in = x_acc.astype(jnp.bfloat16)
    z_in = z_acc.astype(jnp.bfloat16)
    bc_in = bc_acc.astype(jnp.bfloat16)
    joined = jnp.concatenate([x_in, bc_in], axis=1)
    earlier = passed_along(joined[rows_here - (KCONV - 1) :], "seq", 1)
    extended = jnp.concatenate([earlier, joined], axis=0)
    seg_ext = jnp.concatenate(
        [
            segment_of(
                first_row - (KCONV - 1) + jnp.arange(KCONV - 1, dtype=jnp.int32), prompt_end
            ),
            segment,
        ]
    )
    kernel = jnp.concatenate([conv_x, conv_bc], axis=1)
    mixed_in = short_conv(extended, seg_ext, kernel)
    x_conv = mixed_in[:, :width_here].astype(jnp.float32).reshape(rows_here, heads_here, head_width)
    b_conv = mixed_in[:, width_here : width_here + NS].astype(jnp.float32)
    c_conv = mixed_in[:, width_here + NS :].astype(jnp.float32)
    step_size = jax.nn.softplus(dt_raw + dt_bias[None, :])
    log_decay = -decay_rate[None, :] * step_size
    blocks = rows_here // GROUP
    block_first = first_row + jnp.arange(blocks, dtype=jnp.int32) * GROUP
    seg_prior = segment_of(block_first - 1, prompt_end)
    packed = (
        x_conv.reshape(blocks, GROUP, heads_here, head_width),
        b_conv.reshape(blocks, GROUP, NS),
        c_conv.reshape(blocks, GROUP, NS),
        step_size.reshape(blocks, GROUP, heads_here),
        log_decay.reshape(blocks, GROUP, heads_here),
        segment.reshape(blocks, GROUP),
        seg_prior,
    )
    init_state = jnp.zeros((heads_here, head_width, NS), jnp.float32)
    local_end, (outputs, priors) = lax.scan(advance_block, init_state, packed)
    device_prior = seg_prior[0]
    level = jnp.cumsum(log_decay, axis=0)
    through = jnp.where(segment[rows_here - 1] == device_prior, jnp.exp(level[rows_here - 1]), 0.0)

    def link(earlier_pair, later_pair):
        return (
            earlier_pair[0] * later_pair[0],
            later_pair[0][:, None, None] * earlier_pair[1] + later_pair[1],
        )

    unused, entering = prefix(
        (through, local_end), "seq", link, (jnp.ones_like(through), jnp.zeros_like(local_end))
    )
    inflow = jnp.where((segment == device_prior)[:, None], jnp.exp(level), 0.0)
    ssm = outputs.reshape(rows_here, heads_here, head_width)
    ssm = ssm + inflow[:, :, None] * jnp.einsum("in,hpn->ihp", c_conv, entering, precision=highest)
    ssm = ssm + skip_gain[None, :, None] * x_conv
    gated = ssm.reshape(rows_here, width_here) * jax.nn.silu(z_in.astype(jnp.float32))
    square_sum = lax.psum(jnp.sum(gated * gated, axis=1), "tp")
    normed = (gated * lax.rsqrt(square_sum / DIN + epsilon)[:, None] * norm_gain[None, :]).astype(
        jnp.bfloat16
    )
    mixed_cols = lax.psum_scatter(
        lax.dot_general(
            out_weight, normed, (((0,), (1,)), ((), ())), preferred_element_type=jnp.float32
        ),
        "tp",
        scatter_dimension=0,
        tiled=True,
    )
    mixed = mixed_cols.T.astype(jnp.bfloat16)
    last_row = prompt_end - 1
    holder = last_row // rows_here
    present = holder == my_index
    inner = jnp.clip(last_row - first_row, 0, rows_here - 1)

    def finish(prompt_id, inner_row):
        return state_at(
            entering,
            device_prior,
            x_conv,
            b_conv,
            step_size,
            log_decay,
            segment,
            inner_row,
            prompt_id,
        )

    finals = jax.vmap(finish)(jnp.arange(PROMPTS, dtype=jnp.int32), inner)
    finals = jnp.where(present[:, None, None, None], finals, 0.0)

    def edge_of(inner_row, start_row, end_row):
        window = lax.dynamic_slice_in_dim(extended, inner_row + 1, KCONV - 1, 0)
        rows_global = end_row - (KCONV - 2) + jnp.arange(KCONV - 1, dtype=jnp.int32)
        return jnp.where((rows_global >= start_row)[:, None], window, jnp.zeros_like(window))

    edges = jax.vmap(edge_of)(inner, prompt_start, last_row)
    edges = jnp.where(present[:, None, None], edges.astype(jnp.float32), 0.0)
    finals_all, edges_all = lax.psum((finals, edges), "seq")
    keeper = owners[0]
    final_state = finals_all[keeper][None]
    kept_edges = edges_all[keeper]
    conv_edge_x = kept_edges[:, :width_here].astype(jnp.bfloat16)[None]
    conv_edge_bc = kept_edges[:, width_here:].astype(jnp.bfloat16)[None]
    return (mixed, final_state, conv_edge_x, conv_edge_bc)


def solution(mesh):
    return jax.shard_map(
        per_device,
        mesh=mesh,
        in_specs=(
            P("seq", "tp"),
            P(None, "tp"),
            P(None, "tp"),
            P(None, "tp"),
            P(None, "tp"),
            P(None, "tp"),
            P(),
            P("tp"),
            P("tp"),
            P("tp"),
            P("tp"),
            P("tp", None),
            P(),
            P("seq"),
        ),
        out_specs=(
            P("seq", "tp"),
            P("seq", "tp", None, None),
            P("seq", None, "tp"),
            P("seq", None, None),
        ),
        check_vma=False,
    )
```

profile of v0, /device:TPU:1, one launch (start us, length us, event | category | flops | bytes accessed | tf_op | source)
XLA Modules:
  0.0 635.1 jit_solution(17370364813948370289)
XLA Ops:
  12.4 22.5 %all-gather.8.cloned.1.call-done = bf16[2048,256]{0,1:T(8,128)(2,1)} async-done(((bf16[2048,64]{0,1:T(8,128)(2,1)}), bf16[2048,256]{0,1:T(8,128)(2,1)}) %all-gather.8.cloned.1.call-update) | async-done | bytes 1048592 | tf_op jit(solution)/shard_map/all_gather | solution.py:123
  34.9 52.1 %all-gather.6.cloned.1.call-done = bf16[1024,2048]{1,0:T(8,128)(2,1)} async-done(((bf16[1024,512]{1,0:T(8,128)(2,1)}), bf16[1024,2048]{1,0:T(8,128)(2,1)}) %all-gather.6.cloned.1.call-update) | async-done | bytes 4194320 | tf_op jit(solution)/shard_map/all_gather | solution.py:124
  87.0 3.9 convolution_convert_fusion.1
  91.0 7.0 %convolution_convert_fusion = bf16[1024,1024]{0,1:T(8,128)(2,1)S(1)} fusion(bf16[1024,2048]{1,0:T(8,128)(2,1)S(1)} %copy-done.6, bf16[2048,1024]{1,0:T(8,128)(2,1)} %param.19), kind=kOutput, calls=%fused_computation.87 | convolution fusion | flops 4296015872 | bytes 10485760 | tf_op jit(solution)/shard_map/dot_general | solution.py:127
  98.8 3.8 collective-permute-start
  104.0 3.0 collective-permute-done
  107.0 2.8 maximum_maximum_fusion
  109.8 7.4 %multiply_convert_fusion = bf16[1024,1280]{0,1:T(8,128)(2,1)S(1)} fusion(bf16[1024,256]{0,1:T(8,128)(2,1)S(1)} %convolution_convert_fusion.1, bf16[1027,1280]{0,1:T(8,128)(2,1)S(1)} %maximum_maximum_fusion, f32[1280]{0:T(1024)S(1)} %get-tuple-element.304, f32[1024]{0:T(1024)S(1)} %get-tuple-element.360, f32[1280]{0:T(1024)S(1)} %get-tuple-element.305, ...), kind=kLoop, calls=%fused_computation.69 | loop fusion | flops 28835840 | bytes 13139968 | tf_op jit(solution)/shard_map/convert_element_type | solution.py:52
  117.3 1.4 copy-done.5
  118.7 2.4 slice_convert_fusion
  121.6 5.6 reshape_reshape.3
  127.2 162.7 %while.32 = (s32[]{:T(128)}, f32[16,64,128]{2,1,0:T(8,128)S(1)}, f32[4,256,16,64]{1,0,3,2:T(4,128)}, s32[4,256]{1,0:T(4,128)S(1)}, s32[4]{0:T(128)S(1)}, /*index...) while((s32[]{:T(128)}, f32[16,64,128]{2,1,0:T(8,128)S(1)}, ...), condition=%wide.region_7.8_spmd.clone.clone, body=%wide.region_4.7_spmd.clone.sunk.clone | while | flops 1718571520 | bytes 14622798 | solution.py:167
  130.0 1.3 broadcast_compare_fusion.6
  133.1 3.3 constant_dynamic-slice_fusion.14
  136.4 4.9 fusion.121
  144.6 23.4 %dynamic_update_slice.7 = f32[4,256,16,64]{1,0,3,2:T(4,128)} dynamic-update-slice(f32[4,256,16,64]{1,0,3,2:T(4,128)} %get-tuple-element.565, f32[1,256,16,64]{1,0,3,2:T(1,128)S(1)} %copy.168, s32[]{:T(128)S(6)} %copy.175, s32[]{:T(128)} %constant.101.clone.1..sunk.2, s32[]{:T(128)} %constant.101.clone.1..sunk.2, s32[]{:T(128)} %constant.101.clone.1..sunk.2) | dynamic-update-slice | bytes 2097156 | tf_op jit(solution)/shard_map/while/body/jit(dynamic_update_index_in_dim)/dynamic_update_slice | solution.py:167
  170.7 1.3 broadcast_compare_fusion.6
  173.7 3.3 constant_dynamic-slice_fusion.14
  177.0 4.9 fusion.121
  185.3 23.4 %dynamic_update_slice.7 = f32[4,256,16,64]{1,0,3,2:T(4,128)} dynamic-update-slice(f32[4,256,16,64]{1,0,3,2:T(4,128)} %get-tuple-element.565, f32[1,256,16,64]{1,0,3,2:T(1,128)S(1)} %copy.168, s32[]{:T(128)S(6)} %copy.175, s32[]{:T(128)} %constant.101.clone.1..sunk.2, s32[]{:T(128)} %constant.101.clone.1..sunk.2, s32[]{:T(128)} %constant.101.clone.1..sunk.2) | dynamic-update-slice | bytes 2097156 | tf_op jit(solution)/shard_map/while/body/jit(dynamic_update_index_in_dim)/dynamic_update_slice | solution.py:167
  211.3 1.3 broadcast_compare_fusion.6
  214.3 3.3 constant_dynamic-slice_fusion.14
  217.6 4.9 fusion.121
  225.9 23.4 %dynamic_update_slice.7 = f32[4,256,16,64]{1,0,3,2:T(4,128)} dynamic-update-slice(f32[4,256,16,64]{1,0,3,2:T(4,128)} %get-tuple-element.565, f32[1,256,16,64]{1,0,3,2:T(1,128)S(1)} %copy.168, s32[]{:T(128)S(6)} %copy.175, s32[]{:T(128)} %constant.101.clone.1..sunk.2, s32[]{:T(128)} %constant.101.clone.1..sunk.2, s32[]{:T(128)} %constant.101.clone.1..sunk.2) | dynamic-update-slice | bytes 2097156 | tf_op jit(solution)/shard_map/while/body/jit(dynamic_update_index_in_dim)/dynamic_update_slice | solution.py:167
  251.9 1.3 broadcast_compare_fusion.6
  254.9 3.3 constant_dynamic-slice_fusion.14
  258.2 4.9 fusion.121
  266.5 23.4 %dynamic_update_slice.7 = f32[4,256,16,64]{1,0,3,2:T(4,128)} dynamic-update-slice(f32[4,256,16,64]{1,0,3,2:T(4,128)} %get-tuple-element.565, f32[1,256,16,64]{1,0,3,2:T(1,128)S(1)} %copy.168, s32[]{:T(128)S(6)} %copy.175, s32[]{:T(128)} %constant.101.clone.1..sunk.2, s32[]{:T(128)} %constant.101.clone.1..sunk.2, s32[]{:T(128)} %constant.101.clone.1..sunk.2) | dynamic-update-slice | bytes 2097156 | tf_op jit(solution)/shard_map/while/body/jit(dynamic_update_index_in_dim)/dynamic_update_slice | solution.py:167
  293.1 4.5 reduce-window.21
  299.2 24.6 %all-gather.1 = f32[32,1,16]{2,1,0:T(1,128)S(1)} all-gather(f32[1,1,16]{2,1,0:T(1,128)S(1)} %bitcast.252), channel_id=1, replica_groups=mesh['seq'=32,'tp'=4] {'seq'}, dimensions={0}, use_global_device_ids=true | all-gather | bytes 2112 | tf_op jit(solution)/shard_map/all_gather | solution.py:23
  324.0 6.3 reshape.362
  330.4 34.7 %all-gather.10.cloned.1.call-done = f32[512,64,128]{2,1,0:T(8,128)} async-done(((f32[16,64,128]{2,1,0:T(8,128)}), f32[512,64,128]{2,1,0:T(8,128)}) %all-gather.10.cloned.1.call-update) | async-done | bytes 16777232 | tf_op jit(solution)/shard_map/all_gather | solution.py:23
  365.1 37.7 %while.33 = (s32[]{:T(128)}, f32[16,64,128]{2,1,0:T(8,128)S(1)}, s32[]{:T(128)}, f32[32,16]{1,0:T(8,128)S(1)}, f32[32,16,64,128]{3,2,1,0:T(8,128)}) while((s32[]{:T(128)}, f32[16,64,128]{2,1,0:T(8,128)S(1)}, s32[]{:T(128)}, f32[32,16]{1,0:T(8,128)S(1)}, f32[32,16,64,128]{3,2,1,0:T(8,128)}) %tuple.136), condition=%wide.region_11.12_spmd.clone.clone, body=%wide.region_10.11_spmd.clone.sunk.clone | while | flops 524292 | bytes 1573153 | solution.py:32
  402.8 5.9 multiply_add_fusion
  408.8 7.3 %multiply_reduce_fusion = (f32[1024]{0:T(1024)S(1)}, f32[1024,1024]{0,1:T(8,128)}) fusion(bf16[1024,2048]{1,0:T(8,128)(2,1)S(1)} %copy-done.7, bf16[2048,1024]{1,0:T(8,128)(2,1)S(1)} %copy-done.12, f32[1024,16,64]{0,2,1:T(8,128)S(1)} %multiply_add_fusion), kind=kOutput, calls=%fused_computation.76 | convolution fusion | flops 4304403456 | bytes 16781312 | tf_op jit(solution)/shard_map/dot_general | solution.py:127
  416.1 8.5 %psum.21 = f32[1024]{0:T(1024)S(1)} all-reduce(f32[1024]{0:T(1024)S(1)} %get-tuple-element.368), channel_id=1, replica_groups=mesh['seq'=32,'tp'=4] {'tp'}, use_global_device_ids=true, to_apply=%region_13.14 | all-reduce | flops 1024 | bytes 8192 | tf_op jit(solution)/shard_map/psum | solution.py:186
  424.6 11.7 %fusion.47 = f32[4,16,64,128]{3,2,0,1:T(8,128)} fusion(f32[1024,16,64]{0,2,1:T(8,128)} %bitcast.234, f32[1024,16,4]{0,2,1:T(4,128)S(1)} %multiply_bitcast_fusion, f32[16,64,128]{2,1,0:T(8,128)S(1)} %get-tuple-element.153, f32[4,16]{0,1:T(8,128)S(1)} %copy.101, pred[4]{0:T(512)(128)(4,1)S(1)} %fusion.76, bf16[1024,1280]{0,1:T(8,128)(2,1)} %copy-done.5), kind=kOutput, calls=%fused_computation.84 | convolution fusion | flops 6448218112 | bytes 7340292 | tf_op jit(solution)/shard_map/vmap(jh,jhp,jn->hpn)/dot_general | solution.py:92
  436.7 11.4 %convolution_bitcast_fusion = f32[2048,1024]{0,1:T(8,128)} fusion(bf16[1024,2048]{1,0:T(8,128)(2,1)} %param.29, f32[1024,1024]{0,1:T(8,128)} %get-tuple-element.369, f32[1024]{0:T(1024)S(1)} %copy-done.8, f32[1024]{0:T(1024)S(1)} %add_rsqrt_fusion), kind=kOutput, calls=%fused_computation.70 | convolution fusion | flops 4298113024 | bytes 16785408 | tf_op jit(solution)/shard_map/dot_general | solution.py:191
  449.9 3.4 copy.104
  453.3 8.0 %while.31 = (s32[]{:T(128)}, bf16[1027,1280]{1,0:T(8,128)(2,1)}, s32[4,2]{0,1:T(2,128)S(1)}, bf16[4,3,1280]{2,1,0:T(4,128)(2,1)S(1)}) while((s32[]{:T(128)}, bf16[1027,1280]{1,0:T(8,128)(2,1)}, s32[4,2]{0,1:T(2,128)S(1)}, bf16[4,3,1280]{2,1,0:T(4,128)(2,1)S(1)}) %tuple.120), condition=%wide.while_cond.clone, body=%wide.while_body.sunk.clone | while | flops 2 | bytes 18017 | solution.py:221
  453.9 1.4 bitcast_dynamic-update-slice_fusion.3
  455.9 1.4 bitcast_dynamic-update-slice_fusion.3
  457.9 1.4 bitcast_dynamic-update-slice_fusion.3
  459.9 1.4 bitcast_dynamic-update-slice_fusion.3
  461.4 121.7 %psum.23 = bf16[4,3,1280]{2,1,0:T(4,128)(2,1)S(1)} all-reduce(f32[4,3,1280]{2,1,0:T(4,128)S(1)} %convert_select_fusion), channel_id=1, replica_groups=mesh['seq'=32,'tp'=4] {'seq'}, use_global_device_ids=true, to_apply=%region_16.17 | all-reduce | flops 15360 | bytes 92160 | tf_op jit(solution)/shard_map/psum | solution.py:227
  584.3 1.9 dynamic-slice_bitcast_fusion.1
  586.2 39.4 %reduce-scatter.2.cloned.1.call-done = f32[512,1024]{0,1:T(8,128)} async-done(((f32[2048,1024]{0,1:T(8,128)}), f32[512,1024]{0,1:T(8,128)}) %reduce-scatter.2.cloned.1.call-update) | async-done | bytes 2097168 | tf_op jit(solution)/shard_map/reduce_scatter | solution.py:190
  625.6 2.7 convert_bitcast_fusion
  (243 shorter events, 78.5 us)
Async XLA Ops:
  7.2 95.5 %copy-start = (bf16[2048,16]{0,1:T(8,128)(2,1)S(1)}, bf16[2048,16]{0,1:T(8,128)(2,1)}, u32[]{:S(2)}) copy-start(bf16[2048,16]{0,1:T(8,128)(2,1)} %param.22) | copy-start | bytes 196612
  7.2 27.7 %all-gather.8.cloned.1.call-start = ((), (), s32[]{:S(2)}) async-start(), calls=%async_computation.2 | async-start | bytes 1310720 | tf_op jit(solution)/shard_map/all_gather | solution.py:123
  7.9 79.1 %all-gather.6.cloned.1.call-start = ((), (), s32[]{:S(2)}) async-start(), calls=%async_computation.1 | async-start | bytes 5242880 | tf_op jit(solution)/shard_map/all_gather | solution.py:124
  8.7 356.4 %all-gather.10.cloned.1.call-start = ((), (), s32[]{:S(2)}) async-start(), calls=%async_computation.5 | async-start | bytes 17301504 | tf_op jit(solution)/shard_map/all_gather | solution.py:23
  87.0 3.9 copy-start.6
  90.9 11.7 %copy-start.9 = (f32[16]{0:T(128)S(1)}, f32[16]{0:T(128)}, u32[]{:S(2)}) copy-start(f32[16]{0:T(128)} %param.25) | copy-start | bytes 196
  98.8 8.2 %collective-permute-start = (bf16[3,1280]{0,1:T(8,128)(2,1)}, bf16[3,1280]{0,1:T(8,128)(2,1)}, u32[]{:S(2)}, u32[]{:S(2)}) collective-permute-start(bf16[3,1280]{0,1:T(8,128)(2,1)} %fusion.52), channel_id=1, source_target_pairs={{0,4},{4,8},{8,12},{12,16},{16,20},{20,24},{24,28},{28,32},{32,36}... | collective-permute-start | bytes 23048 | tf_op jit(solution)/shard_map/ppermute | solution.py:18
  109.8 7.4 %copy-start.2 = (bf16[1027,1280]{0,1:T(8,128)(2,1)}, bf16[1027,1280]{0,1:T(8,128)(2,1)S(1)}, u32[]{:S(2)}) copy-start(bf16[1027,1280]{0,1:T(8,128)(2,1)S(1)} %maximum_maximum_fusion) | copy-start | bytes 7887364
  117.2 1.5 copy-start.5
  127.2 165.7 %copy-start.10 = (s32[4]{0:T(128)S(1)}, s32[4]{0:T(128)}, u32[]{:S(2)}) copy-start(s32[4]{0:T(128)} %param.30) | copy-start | bytes 52
  289.9 0.8 copy-start.4
  290.7 293.6 %all-reduce.4.cloned.1.call-start = ((), (), s32[]{:S(2)}) async-start(), calls=%async_computation.4 | async-start | bytes 4194304 | tf_op jit(solution)/shard_map/psum | solution.py:227
  330.4 72.4 %copy-start.11 = (f32[16]{0:T(128)S(1)}, f32[16]{0:T(128)}, u32[]{:S(2)}) copy-start(f32[16]{0:T(128)} %param.27) | copy-start | bytes 196
  402.8 5.9 copy-start.7
  402.8 6.0 copy-start.12
  424.6 12.0 %copy-start.8 = (f32[1024]{0:T(1024)S(1)}, f32[1024]{0:T(1024)}, u32[]{:S(2)}) copy-start(f32[1024]{0:T(1024)} %param.28) | copy-start | bytes 12292
  436.4 189.2 %reduce-scatter.2.cloned.1.call-start = ((), (), s32[]{:S(2)}) async-start(), calls=%async_computation.3 | async-start | bytes 10485760 | tf_op jit(solution)/shard_map/reduce_scatter | solution.py:190
  448.0 1.9 copy-start.3
  448.9 179.4 %copy-start.1 = (bf16[2048,16]{0,1:T(8,128)(2,1)S(1)}, bf16[2048,16]{0,1:T(8,128)(2,1)}, u32[]{:S(2)}) copy-start(bf16[2048,16]{0,1:T(8,128)(2,1)} %param.22) | copy-start | bytes 196612
Sparse Core Ops, SparseCore 0:
  9.7 25.1 all-gather.7
  36.5 50.4 all-gather.5
  290.9 74.1 all-gather.9
  436.5 106.7 all-reduce.3
  545.6 79.9 reduce-scatter.1
where the time goes:
time: 647 us; the launch traced here: 635 us
  blocking collectives  155 us (24%)
  waiting for transfers between devices  153 us (24%)
  local copies, waits for them, and re-layouts  152 us (23%)
  matrix products  78.5 us (12%)
  other arithmetic  69.2 us (11%)
  between operations  15.9 us (2%)
  loops' own time  7.02 us (1%)
    psum x1, blocking collectives, per_device(): finals_all, edges_all = lax.psum((finals, edges), 'seq')  122 us
    dynamic_update_slice x8, local copies, waits for them, and re-layouts, per_device(): local_end, (outputs, priors) = lax.scan(advance_block, init_state, packed)  98.1 us
    all_gather x1, waiting for transfers between devices, per_device(): piece = lax.all_gather(hidden, 'tp', axis=1, tiled=True)  52.1 us
    reduce_scatter x1, waiting for transfers between devices, per_device(): lax.psum_scatter(lax.dot_general(out_weight, normed, (((0,), (1,)), ((),...  39.4 us
    select_n x31, other arithmetic, lap(): jnp.where(position < mine, new, old)  36.4 us
    all_gather x1, waiting for transfers between devices, prefix(): pieces = jax.tree.map(lambda part: lax.all_gather(part, axis), value)  34.7 us
    all_gather x1, blocking collectives, prefix(): pieces = jax.tree.map(lambda part: lax.all_gather(part, axis), value)  24.6 us
    all_gather x1, waiting for transfers between devices, per_device(): bc_full = lax.all_gather(bc_weight, 'tp', axis=1, tiled=True)  22.5 us
  transfers between devices with their start and end apart: 6, of which 5 were waited for; matrix products, arithmetic and copies ran while one was open for 7% of the time, Pallas kernels for 0%

commit v1 on v0

--- a/solution.py
+++ b/solution.py
@@ -2,6 +2,7 @@
 import jax.numpy as jnp
 from jax import lax
 from jax.sharding import PartitionSpec as P
+from jax.lax import all_to_all, axis_size
 
 NS = 128
 KCONV = 4
@@ -120,7 +121,12 @@
     prompt_start = prompt_end - lengths
     positions = first_row + jnp.arange(rows_here, dtype=jnp.int32)
     segment = segment_of(positions, prompt_end)
-    bc_full = lax.all_gather(bc_weight, "tp", axis=1, tiled=True)
+    heap = []
+    for _ in range(axis_size("tp")):
+        heap.append(bc_weight)
+    state_now = jnp.stack(heap, axis=0)
+    item_now = all_to_all(state_now, split_axis=0, concat_axis=0, axis_name="tp")
+    bc_full = jnp.concatenate(item_now, axis=1)
     piece = lax.all_gather(hidden, "tp", axis=1, tiled=True)
 
     def take(matrix):

time: 647 us -> 624 us (0.964)
  waiting for transfers between devices: 153 us -> 125 us
    all_gather x1 -> x0, waiting for transfers between devices: 22.5 us -> none  [per_device(): bc_full = lax.all_gather(bc_weight, 'tp', axis=1, tiled=True)]
    all_gather x1, waiting for transfers between devices: 52.1 us -> 34 us  [per_device(): piece = lax.all_gather(hidden, 'tp', axis=1, tiled=True)]
    all_to_all x0 -> x1, waiting for transfers between devices: none -> 14.7 us  [per_device(): all_to_all(state_now, split_axis=0, concat_axis=0, axis_name='tp')]
where the time goes in v1:
time: 624 us; the launch traced here: 612 us
  blocking collectives  156 us (25%)
  local copies, waits for them, and re-layouts  153 us (25%)
  waiting for transfers between devices  125 us (20%)
  matrix products  78.3 us (13%)
  other arithmetic  67.8 us (11%)
  between operations  16 us (3%)
  starting transfers between devices  8.74 us (1%)
  loops' own time  6.92 us (1%)
    psum x1, blocking collectives, per_device(): finals_all, edges_all = lax.psum((finals, edges), 'seq')  122 us
    dynamic_update_slice x8, local copies, waits for them, and re-layouts, per_device(): local_end, (outputs, priors) = lax.scan(advance_block, init_state, packed)  98.1 us
    reduce_scatter x1, waiting for transfers between devices, per_device(): lax.psum_scatter(lax.dot_general(out_weight, normed, (((0,), (1,)), ((),...  39.4 us
    select_n x31, other arithmetic, lap(): jnp.where(position < mine, new, old)  36.4 us
    all_gather x1, waiting for transfers between devices, per_device(): piece = lax.all_gather(hidden, 'tp', axis=1, tiled=True)  34 us
    all_gather x1, waiting for transfers between devices, prefix(): pieces = jax.tree.map(lambda part: lax.all_gather(part, axis), value)  33.6 us
    all_gather x1, blocking collectives, prefix(): pieces = jax.tree.map(lambda part: lax.all_gather(part, axis), value)  25.6 us
    dot_general x4, matrix products, advance_block(): output = jnp.einsum('ijh,jhp->ihp', mixing, x_blk, precision=highest)  19.7 us
  transfers between devices with their start and end apart: 6, of which 5 were waited for; matrix products, arithmetic and copies ran while one was open for 7% of the time, Pallas kernels for 0%

profile of v1, /device:TPU:1, one launch (start us, length us, event | category | flops | bytes accessed | tf_op | source)
XLA Modules:
  0.0 611.7 jit_solution(8621752966474387888)
XLA Ops:
  8.0 2.0 stack.2
  10.0 4.8 all-to-all-start
  15.8 14.7 %all-to-all-done = bf16[4,2048,64]{1,2,0:T(8,128)(2,1)S(1)} async-done(((bf16[4,2048,64]{1,2,0:T(8,128)(2,1)}), bf16[4,2048,64]{1,2,0:T(8,128)(2,1)S(1)}, u32[]{:S(2)}, u32[]{:S(2)}) %all-to-all-start) | async-done | bytes 1048608 | tf_op jit(solution)/shard_map/all_to_all | solution.py:128
  30.5 34.0 %all-gather.5.cloned.1.call-done = bf16[1024,2048]{1,0:T(8,128)(2,1)} async-done(((bf16[1024,512]{1,0:T(8,128)(2,1)}), bf16[1024,2048]{1,0:T(8,128)(2,1)}) %all-gather.5.cloned.1.call-update) | async-done | bytes 4194320 | tf_op jit(solution)/shard_map/all_gather | solution.py:130
  64.4 3.7 convolution_convert_fusion.1
  68.2 7.0 %convolution_convert_fusion = bf16[1024,1024]{0,1:T(8,128)(2,1)S(1)} fusion(bf16[1024,2048]{1,0:T(8,128)(2,1)S(1)} %copy-done.6, bf16[2048,1024]{1,0:T(8,128)(2,1)} %param.19), kind=kOutput, calls=%fused_computation.87 | convolution fusion | flops 4296015872 | bytes 10485760 | tf_op jit(solution)/shard_map/dot_general | solution.py:133
  76.1 3.6 collective-permute-start
  81.0 3.0 collective-permute-done
  84.0 2.8 maximum_maximum_fusion
  86.8 7.4 %multiply_convert_fusion = bf16[1024,1280]{0,1:T(8,128)(2,1)S(1)} fusion(bf16[1024,256]{0,1:T(8,128)(2,1)S(1)} %convolution_convert_fusion.1, bf16[1027,1280]{0,1:T(8,128)(2,1)S(1)} %maximum_maximum_fusion, f32[1280]{0:T(1024)S(1)} %get-tuple-element.304, f32[1024]{0:T(1024)S(1)} %get-tuple-element.360, f32[1280]{0:T(1024)S(1)} %get-tuple-element.305, ...), kind=kLoop, calls=%fused_computation.69 | loop fusion | flops 28835840 | bytes 13139968 | tf_op jit(solution)/shard_map/convert_element_type | solution.py:53
  94.3 1.4 copy-done.5
  95.7 2.4 slice_convert_fusion
  98.6 5.6 reshape_reshape.3
  104.2 162.3 %while.32 = (s32[]{:T(128)}, f32[16,64,128]{2,1,0:T(8,128)S(1)}, f32[4,256,16,64]{1,0,3,2:T(4,128)}, s32[4,256]{1,0:T(4,128)S(1)}, s32[4]{0:T(128)S(1)}, /*index...) while((s32[]{:T(128)}, f32[16,64,128]{2,1,0:T(8,128)S(1)}, ...), condition=%wide.region_7.8_spmd.clone.clone, body=%wide.region_4.7_spmd.clone.sunk.clone | while | flops 1718571520 | bytes 14622798 | solution.py:173
  107.0 1.3 broadcast_compare_fusion.6
  110.0 3.3 constant_dynamic-slice_fusion.14
  113.3 4.9 fusion.121
  121.5 23.4 %dynamic_update_slice.7 = f32[4,256,16,64]{1,0,3,2:T(4,128)} dynamic-update-slice(f32[4,256,16,64]{1,0,3,2:T(4,128)} %get-tuple-element.565, f32[1,256,16,64]{1,0,3,2:T(1,128)S(1)} %copy.169, s32[]{:T(128)S(6)} %copy.176, s32[]{:T(128)} %constant.101.clone.1..sunk.2, s32[]{:T(128)} %constant.101.clone.1..sunk.2, s32[]{:T(128)} %constant.101.clone.1..sunk.2) | dynamic-update-slice | bytes 2097156 | tf_op jit(solution)/shard_map/while/body/jit(dynamic_update_index_in_dim)/dynamic_update_slice | solution.py:173
  147.5 1.3 broadcast_compare_fusion.6
  150.5 3.3 constant_dynamic-slice_fusion.14
  153.8 4.9 fusion.121
  162.0 23.4 %dynamic_update_slice.7 = f32[4,256,16,64]{1,0,3,2:T(4,128)} dynamic-update-slice(f32[4,256,16,64]{1,0,3,2:T(4,128)} %get-tuple-element.565, f32[1,256,16,64]{1,0,3,2:T(1,128)S(1)} %copy.169, s32[]{:T(128)S(6)} %copy.176, s32[]{:T(128)} %constant.101.clone.1..sunk.2, s32[]{:T(128)} %constant.101.clone.1..sunk.2, s32[]{:T(128)} %constant.101.clone.1..sunk.2) | dynamic-update-slice | bytes 2097156 | tf_op jit(solution)/shard_map/while/body/jit(dynamic_update_index_in_dim)/dynamic_update_slice | solution.py:173
  191.0 3.3 constant_dynamic-slice_fusion.14
  194.3 4.9 fusion.121
  202.5 23.4 %dynamic_update_slice.7 = f32[4,256,16,64]{1,0,3,2:T(4,128)} dynamic-update-slice(f32[4,256,16,64]{1,0,3,2:T(4,128)} %get-tuple-element.565, f32[1,256,16,64]{1,0,3,2:T(1,128)S(1)} %copy.169, s32[]{:T(128)S(6)} %copy.176, s32[]{:T(128)} %constant.101.clone.1..sunk.2, s32[]{:T(128)} %constant.101.clone.1..sunk.2, s32[]{:T(128)} %constant.101.clone.1..sunk.2) | dynamic-update-slice | bytes 2097156 | tf_op jit(solution)/shard_map/while/body/jit(dynamic_update_index_in_dim)/dynamic_update_slice | solution.py:173
  231.5 3.3 constant_dynamic-slice_fusion.14
  234.8 4.9 fusion.121
  243.0 23.4 %dynamic_update_slice.7 = f32[4,256,16,64]{1,0,3,2:T(4,128)} dynamic-update-slice(f32[4,256,16,64]{1,0,3,2:T(4,128)} %get-tuple-element.565, f32[1,256,16,64]{1,0,3,2:T(1,128)S(1)} %copy.169, s32[]{:T(128)S(6)} %copy.176, s32[]{:T(128)} %constant.101.clone.1..sunk.2, s32[]{:T(128)} %constant.101.clone.1..sunk.2, s32[]{:T(128)} %constant.101.clone.1..sunk.2) | dynamic-update-slice | bytes 2097156 | tf_op jit(solution)/shard_map/while/body/jit(dynamic_update_index_in_dim)/dynamic_update_slice | solution.py:173
  269.6 4.5 reduce-window.21
  275.8 25.6 %all-gather.1 = f32[32,1,16]{2,1,0:T(1,128)S(1)} all-gather(f32[1,1,16]{2,1,0:T(1,128)S(1)} %bitcast.256), channel_id=1, replica_groups=mesh['seq'=32,'tp'=4] {'seq'}, dimensions={0}, use_global_device_ids=true | all-gather | bytes 2112 | tf_op jit(solution)/shard_map/all_gather | solution.py:24
  301.5 6.5 %reshape.372 = f32[1024,16,64]{0,2,1:T(8,128)} reshape(f32[4,256,16,64]{1,0,3,2:T(4,128)} %get-tuple-element.151) | data formatting | bytes 8388608 | tf_op jit(solution)/shard_map/reshape | solution.py:188
  308.1 33.6 %all-gather.7.cloned.1.call-done = f32[512,64,128]{2,1,0:T(8,128)} async-done(((f32[16,64,128]{2,1,0:T(8,128)}), f32[512,64,128]{2,1,0:T(8,128)}) %all-gather.7.cloned.1.call-update) | async-done | bytes 16777232 | tf_op jit(solution)/shard_map/all_gather | solution.py:24
  341.7 37.7 %while.33 = (s32[]{:T(128)}, f32[16,64,128]{2,1,0:T(8,128)S(1)}, s32[]{:T(128)}, f32[32,16]{1,0:T(8,128)S(1)}, f32[32,16,64,128]{3,2,1,0:T(8,128)}) while((s32[]{:T(128)}, f32[16,64,128]{2,1,0:T(8,128)S(1)}, s32[]{:T(128)}, f32[32,16]{1,0:T(8,128)S(1)}, f32[32,16,64,128]{3,2,1,0:T(8,128)}) %tuple.134), condition=%wide.region_11.12_spmd.clone.clone, body=%wide.region_10.11_spmd.clone.sunk.clone | while | flops 524292 | bytes 1573153 | solution.py:33
  379.5 5.9 multiply_add_fusion
  385.4 7.3 %multiply_reduce_fusion = (f32[1024]{0:T(1024)S(1)}, f32[1024,1024]{0,1:T(8,128)}) fusion(bf16[1024,2048]{1,0:T(8,128)(2,1)S(1)} %copy-done.7, bf16[2048,1024]{1,0:T(8,128)(2,1)S(1)} %copy-done.14, f32[1024,16,64]{0,2,1:T(8,128)S(1)} %multiply_add_fusion), kind=kOutput, calls=%fused_computation.76 | convolution fusion | flops 4304403456 | bytes 16781312 | tf_op jit(solution)/shard_map/dot_general | solution.py:133
  392.7 8.5 %psum.21 = f32[1024]{0:T(1024)S(1)} all-reduce(f32[1024]{0:T(1024)S(1)} %get-tuple-element.368), channel_id=1, replica_groups=mesh['seq'=32,'tp'=4] {'tp'}, use_global_device_ids=true, to_apply=%region_13.14 | all-reduce | flops 1024 | bytes 8192 | tf_op jit(solution)/shard_map/psum | solution.py:192
  401.3 11.7 %fusion.47 = f32[4,16,64,128]{3,2,0,1:T(8,128)} fusion(f32[1024,16,64]{0,2,1:T(8,128)} %bitcast.237, f32[1024,16,4]{0,2,1:T(4,128)S(1)} %multiply_bitcast_fusion, f32[16,64,128]{2,1,0:T(8,128)S(1)} %get-tuple-element.153, f32[4,16]{0,1:T(8,128)S(1)} %copy.102, pred[4]{0:T(512)(128)(4,1)S(1)} %fusion.76, bf16[1024,1280]{0,1:T(8,128)(2,1)} %copy-done.5), kind=kOutput, calls=%fused_computation.84 | convolution fusion | flops 6448218112 | bytes 7340292 | tf_op jit(solution)/shard_map/vmap(jh,jhp,jn->hpn)/dot_general | solution.py:93
  413.3 11.4 %convolution_bitcast_fusion = f32[2048,1024]{0,1:T(8,128)} fusion(bf16[1024,2048]{1,0:T(8,128)(2,1)} %param.29, f32[1024,1024]{0,1:T(8,128)} %get-tuple-element.369, f32[1024]{0:T(1024)S(1)} %copy-done.8, f32[1024]{0:T(1024)S(1)} %add_rsqrt_fusion), kind=kOutput, calls=%fused_computation.70 | convolution fusion | flops 4298113024 | bytes 16785408 | tf_op jit(solution)/shard_map/dot_general | solution.py:197
  426.5 3.4 copy.105
  429.9 8.0 %while.31 = (s32[]{:T(128)}, bf16[1027,1280]{1,0:T(8,128)(2,1)}, s32[4,2]{0,1:T(2,128)S(1)}, bf16[4,3,1280]{2,1,0:T(4,128)(2,1)S(1)}) while((s32[]{:T(128)}, bf16[1027,1280]{1,0:T(8,128)(2,1)}, s32[4,2]{0,1:T(2,128)S(1)}, bf16[4,3,1280]{2,1,0:T(4,128)(2,1)S(1)}) %tuple.120), condition=%wide.while_cond.clone, body=%wide.while_body.sunk.clone | while | flops 2 | bytes 18017 | solution.py:227
  430.5 1.4 bitcast_dynamic-update-slice_fusion.3
  432.5 1.4 bitcast_dynamic-update-slice_fusion.3
  434.5 1.4 bitcast_dynamic-update-slice_fusion.3
  436.5 1.4 bitcast_dynamic-update-slice_fusion.3
  438.0 121.7 %psum.23 = bf16[4,3,1280]{2,1,0:T(4,128)(2,1)S(1)} all-reduce(f32[4,3,1280]{2,1,0:T(4,128)S(1)} %convert_select_fusion), channel_id=1, replica_groups=mesh['seq'=32,'tp'=4] {'seq'}, use_global_device_ids=true, to_apply=%region_16.17 | all-reduce | flops 15360 | bytes 92160 | tf_op jit(solution)/shard_map/psum | solution.py:233
  560.9 1.9 dynamic-slice_bitcast_fusion.1
  562.8 39.4 %reduce-scatter.2.cloned.1.call-done = f32[512,1024]{0,1:T(8,128)} async-done(((f32[2048,1024]{0,1:T(8,128)}), f32[512,1024]{0,1:T(8,128)}) %reduce-scatter.2.cloned.1.call-update) | async-done | bytes 2097168 | tf_op jit(solution)/shard_map/reduce_scatter | solution.py:196
  602.2 2.7 convert_bitcast_fusion
  (249 shorter events, 77.4 us)
Async XLA Ops:
  7.2 72.5 %copy-start = (bf16[2048,16]{0,1:T(8,128)(2,1)S(1)}, bf16[2048,16]{0,1:T(8,128)(2,1)}, u32[]{:S(2)}) copy-start(bf16[2048,16]{0,1:T(8,128)(2,1)} %param.22) | copy-start | bytes 196612
  7.2 7.7 %copy-start.12 = (s32[4]{0:T(128)S(1)}, s32[4]{0:T(128)}, u32[]{:S(2)}) copy-start(s32[4]{0:T(128)} %param.30) | copy-start | bytes 52
  7.2 7.8 %copy-start.15 = (f32[16]{0:T(128)S(1)}, f32[16]{0:T(128)}, u32[]{:S(2)}) copy-start(f32[16]{0:T(128)} %param.26) | copy-start | bytes 196
  7.2 8.0 %copy-start.9 = (f32[4,1024]{1,0:T(4,128)S(1)}, f32[4,1024]{1,0:T(4,128)}, u32[]{:S(2)}) copy-start(f32[4,1024]{1,0:T(4,128)} %param.23) | copy-start | bytes 49156
  7.2 8.0 %copy-start.10 = (f32[4,256]{1,0:T(4,128)S(1)}, f32[4,256]{1,0:T(4,128)}, u32[]{:S(2)}) copy-start(f32[4,256]{1,0:T(4,128)} %param.24) | copy-start | bytes 12292
  7.2 57.2 %all-gather.5.cloned.1.call-start = ((), (), s32[]{:S(2)}) async-start(), calls=%async_computation.2 | async-start | bytes 5242880 | tf_op jit(solution)/shard_map/all_gather | solution.py:130
  10.0 20.5 %all-to-all-start = ((bf16[4,2048,64]{1,2,0:T(8,128)(2,1)}), bf16[4,2048,64]{1,2,0:T(8,128)(2,1)S(1)}, u32[]{:S(2)}, u32[]{:S(2)}) async-start(bf16[4,2048,64]{1,2,0:T(8,128)(2,1)} %stack.2), calls=%async_computation | async-start | bytes 2097152 | tf_op jit(solution)/shard_map/all_to_all | solution.py:128
  14.8 326.9 %all-gather.7.cloned.1.call-start = ((), (), s32[]{:S(2)}) async-start(), calls=%async_computation.5 | async-start | bytes 17301504 | tf_op jit(solution)/shard_map/all_gather | solution.py:24
  64.4 3.8 copy-start.6
  68.2 11.5 %copy-start.11 = (f32[16]{0:T(128)S(1)}, f32[16]{0:T(128)}, u32[]{:S(2)}) copy-start(f32[16]{0:T(128)} %param.25) | copy-start | bytes 196
  76.1 7.9 %collective-permute-start = (bf16[3,1280]{0,1:T(8,128)(2,1)}, bf16[3,1280]{0,1:T(8,128)(2,1)}, u32[]{:S(2)}, u32[]{:S(2)}) collective-permute-start(bf16[3,1280]{0,1:T(8,128)(2,1)} %fusion.52), channel_id=1, source_target_pairs={{0,4},{4,8},{8,12},{12,16},{16,20},{20,24},{24,28},{28,32},{32,36}... | collective-permute-start | bytes 23048 | tf_op jit(solution)/shard_map/ppermute | solution.py:19
  86.8 7.4 %copy-start.2 = (bf16[1027,1280]{0,1:T(8,128)(2,1)}, bf16[1027,1280]{0,1:T(8,128)(2,1)S(1)}, u32[]{:S(2)}) copy-start(bf16[1027,1280]{0,1:T(8,128)(2,1)S(1)} %maximum_maximum_fusion) | copy-start | bytes 7887364
  94.2 1.5 copy-start.5
  266.5 0.8 copy-start.4
  267.3 293.6 %all-reduce.4.cloned.1.call-start = ((), (), s32[]{:S(2)}) async-start(), calls=%async_computation.4 | async-start | bytes 4194304 | tf_op jit(solution)/shard_map/psum | solution.py:233
  308.1 71.4 %copy-start.13 = (f32[16]{0:T(128)S(1)}, f32[16]{0:T(128)}, u32[]{:S(2)}) copy-start(f32[16]{0:T(128)} %param.27) | copy-start | bytes 196
  379.4 5.9 copy-start.7
  379.4 6.0 copy-start.14
  401.2 12.0 %copy-start.8 = (f32[1024]{0:T(1024)S(1)}, f32[1024]{0:T(1024)}, u32[]{:S(2)}) copy-start(f32[1024]{0:T(1024)} %param.28) | copy-start | bytes 12292
  413.0 189.2 %reduce-scatter.2.cloned.1.call-start = ((), (), s32[]{:S(2)}) async-start(), calls=%async_computation.3 | async-start | bytes 10485760 | tf_op jit(solution)/shard_map/reduce_scatter | solution.py:196
  424.7 1.9 copy-start.3
  425.5 179.4 %copy-start.1 = (bf16[2048,16]{0,1:T(8,128)(2,1)S(1)}, bf16[2048,16]{0,1:T(8,128)(2,1)}, u32[]{:S(2)}) copy-start(bf16[2048,16]{0,1:T(8,128)(2,1)} %param.22) | copy-start | bytes 196612
Sparse Core Ops, SparseCore 0:
  9.7 54.6 all-gather.4
  267.4 74.2 all-gather.6
  413.1 106.6 all-reduce.3
  522.2 80.0 reduce-scatter.1
